TPU v7x, 256 devices: a whole 4x4x8 slice. The times are simulated.
256 devices in a mesh: pair: 128 (over x, z, y), aux: 2 (over core).
Axes of the slice: x: 4, y: 4, z: 8, core: 2. Of those that a mesh axis runs over, the one named last changes fastest.
Arguments:
- amplitudes: bfloat16 [16384, 128, 128], P('pair', 'aux'), may hold values from -6 to 6
- k_term: bfloat16 [16384, 128, 128], P('pair', 'aux'), may hold values from -6 to 6
- margin_table: bfloat16 [1024, 128, 128], P('pair'), may hold values from -0.5 to 0.5
- margin_index: int32 [16384], P('pair'), may hold values from 0 to 7
- factors: bfloat16 [128, 512, 128], P('pair', 'aux'), may hold values from -6 to 6
- vir_energy: float32 [16384, 128], P('pair'), may hold values from 0.5 to 3
- occ_energy: float32 [128], replicated, may hold values from -2 to -0.3
- pair_owner: int32 [16384, 1], P('pair'), may hold values from 0 to 127; in each aligned block of 128 rows (0 to 127, 128 to 255, ...) at most 2 rows name the same one
Outputs:
- updated: bfloat16 [16384, 128, 128], P('pair', 'aux')
Inputs may be any that keep to these rules, and one draw needn't show every extreme that they name: `pair_owner`: no more than 2 of the 128 pairs of one aligned block name the same owner. `margin_index`: an index into the 8 margin blocks that belong to the pair's aligned block of 128 pairs.
All inputs are finite; a program needn't handle non-finite values.
Results may differ from a plain program's by a relative error of at most 0.0055.
Values may be sent and summed in bfloat16 or wider, within the bound.
No kernel may reach another device: no remote copies, remote signals or barrier semaphores. Data moves between devices by JAX's collectives and lax.ppermute only.
A program may use at most 128 MiB of HBM per device.

v0:
```python
import jax
import jax.numpy as jnp
from jax import lax
from jax.sharding import PartitionSpec as P

RING_ORDER = ((8, 4), (4, 1), (4, 32))


def ring_gather(block, size, stride, total):
    pieces = [block]
    for shift in range(1, size):
        perm = []
        for device in range(total):
            coord = device // stride % size
            perm.append((device, device + ((coord + shift) % size - coord) * stride))
        pieces.append(lax.ppermute(block, "pair", perm))
    return jnp.stack(pieces)


def local(
    amplitudes, k_term, margin_table, margin_index, factors, vir_energy, occ_energy, pair_owner
):
    axis_pairs = lax.axis_size("pair")
    aux_count = lax.axis_size("aux")
    own_index = lax.axis_index("pair")
    aux_index = lax.axis_index("aux")
    pair_count = amplitudes.shape[0]
    row_count = amplitudes.shape[1]
    vir_width = amplitudes.shape[2]
    aux_rows = factors.shape[1]
    ovl_count = margin_table.shape[0]
    cycle_scale = float(vir_width * aux_rows * aux_count * pair_count) ** (-0.5)
    every_factor = lax.all_gather(factors[0], ("pair", "aux"), axis=0, tiled=True)
    every_factor = every_factor.reshape(axis_pairs, aux_count * aux_rows, vir_width)
    own_factors = lax.dynamic_index_in_dim(every_factor, own_index, 0, keepdims=False)
    other_amp = lax.ppermute(amplitudes, "aux", perm=[(0, 1), (1, 0)])
    full_amp = jnp.where(
        aux_index == 0,
        jnp.concatenate([amplitudes, other_amp], axis=1),
        jnp.concatenate([other_amp, amplitudes], axis=1),
    )
    block_pick = (margin_index[:, None] == jnp.arange(ovl_count, dtype=jnp.int32)[None, :]).astype(
        jnp.bfloat16
    )
    margin = jnp.einsum(
        "po,oab->pab", block_pick, margin_table, preferred_element_type=jnp.float32
    ).astype(jnp.bfloat16)
    halfway = jnp.einsum(
        "pca,pab->pcb", full_amp, margin, preferred_element_type=jnp.float32
    ).astype(jnp.bfloat16)
    rotated = jnp.einsum(
        "pac,pab->pcb", margin, halfway, preferred_element_type=jnp.float32
    ).astype(jnp.bfloat16)
    rotated = lax.dynamic_slice_in_dim(rotated, aux_index * row_count, row_count, 1)
    pair_dest = pair_owner[:, 0]
    owner_pick = (jnp.arange(axis_pairs, dtype=jnp.int32)[:, None] == pair_dest[None, :]).astype(
        jnp.bfloat16
    )
    outgoing = jnp.einsum(
        "jp,pcb->jcb", owner_pick, rotated, preferred_element_type=jnp.float32
    ).astype(jnp.bfloat16)
    occ_sum = occ_energy[own_index] + occ_energy[pair_dest]
    energy_rows = lax.dynamic_slice_in_dim(vir_energy, aux_index * row_count, row_count, 1)
    denominator = energy_rows[:, :, None] + vir_energy[:, None, :] - occ_sum[:, None, None]
    inverse = 1.0 / denominator
    prior = amplitudes.astype(jnp.float32) - k_term.astype(jnp.float32) * inverse
    outgoing, prior, inverse = lax.optimization_barrier((outgoing, prior, inverse))
    incoming = lax.all_to_all(outgoing, "pair", 0, 0, tiled=True)
    dressed = jnp.einsum(
        "ica,iqa->cq", incoming, every_factor, preferred_element_type=jnp.float32
    ).astype(jnp.bfloat16)
    local_cycle = jnp.dot(dressed, own_factors, preferred_element_type=jnp.float32)
    cycle_vals = (cycle_scale * local_cycle).astype(jnp.bfloat16)
    returned = cycle_vals
    ring_offset = jnp.zeros_like(pair_dest)
    ring_scale = 1
    for size, stride in RING_ORDER:
        returned = ring_gather(returned, size, stride, axis_pairs)
        own_coord = own_index // stride % size
        dest_coord = pair_dest // stride % size
        ring_offset = ring_offset + (own_coord - dest_coord) % size * ring_scale
        ring_scale = ring_scale * size
    returned = returned.reshape(axis_pairs, row_count, vir_width)
    offset_pick = (jnp.arange(axis_pairs, dtype=jnp.int32)[:, None] == ring_offset[None, :]).astype(
        jnp.bfloat16
    )
    own_cycle = jnp.einsum(
        "jp,jca->pca", offset_pick, returned, preferred_element_type=jnp.float32
    ).astype(jnp.bfloat16)
    cycle_term = jnp.einsum("pca,pba->pcb", own_cycle, margin, preferred_element_type=jnp.float32)
    updated = prior - cycle_term * inverse
    return updated.astype(jnp.bfloat16)


def solution(mesh):
    placed = (
        P("pair", "aux", None),
        P("pair", "aux", None),
        P("pair", None, None),
        P("pair"),
        P("pair", "aux", None),
        P("pair", None),
        P(),
        P("pair", None),
    )
    return jax.shard_map(
        local, mesh=mesh, in_specs=placed, out_specs=P("pair", "aux", None), check_vma=False
    )
```

profile of v0, /device:TPU:3, one launch (start us, length us, event | category | flops | bytes accessed | tf_op | source)
XLA Modules:
  0.0 224.5 jit_solution(11171059530084323425)
XLA Ops:
  8.0 1.2 dynamic_slice.15
  9.9 1.6 gather_fusion
  11.5 1.1 constant_dynamic-slice_fusion
  13.3 3.9 %convolution_convert_fusion = bf16[128,128,128]{2,0,1:T(8,128)(2,1)} fusion(bf16[8,128,128]{2,1,0:T(8,128)(2,1)S(1)} %copy-done, s32[128]{0:T(128)} %param.11), kind=kOutput, calls=%fused_computation.19 | convolution fusion | flops 35652608 | bytes 4456960 | tf_op jit(solution)/shard_map/po,oab->pab/dot_general | solution.py:45
  17.2 4.8 %subtract_divide_fusion = (f32[128,64,128]{2,1,0:T(8,128)}, f32[128,64,128]{2,1,0:T(8,128)}) fusion(f32[128]{0:T(128)S(1)} %broadcast_add_fusion, f32[128,128]{1,0:T(8,128)S(1)} %copy-done.5, f32[128,64]{1,0:T(8,128)S(1)} %constant_dynamic-slice_fusion, bf16[128,64,128]{2,1,0:T(8,128)(2,1)S(1)} %copy-done.3, bf16[128,64,128]{2,1,0:T(8,128)(2,1)S(1)} %copy-done.4), kind=kLoop, calls=%fused_computation.11 | loop fusion | flops 7340032 | bytes 12681728 | tf_op jit(solution)/shard_map/div | solution.py:65
  22.0 14.9 %fusion.6 = bf16[128,128,128]{2,1,0:T(8,128)(2,1)} fusion(bf16[128,128,128]{2,0,1:T(8,128)(2,1)} %convolution_convert_fusion, bf16[128,64,128]{2,1,0:T(8,128)(2,1)} %collective-permute-done, bf16[128,64,128]{2,1,0:T(8,128)(2,1)} %param.8, pred[]{:T(512)S(6)} %eq.62), kind=kOutput, calls=%fused_computation.12 | convolution fusion | flops 1094713344 | bytes 12582913 | tf_op jit(solution)/shard_map/pac,pab->pcb/dot_general | solution.py:51
  36.9 1.8 dynamic-slice_convert_fusion
  38.7 1.8 fusion.22
  40.4 1.4 copy.17
  41.8 70.9 %all_to_all.5 = bf16[128,64,128]{2,1,0:T(8,128)(2,1)S(1)} all-to-all(bf16[128,64,128]{2,1,0:T(8,128)(2,1)S(1)} %copy.17), channel_id=1, replica_groups=mesh['pair'=128,'aux'=2] {'pair'}, dimensions={0} | all-to-all | bytes 4194304 | tf_op jit(solution)/shard_map/all_to_all | solution.py:68
  112.7 32.9 %all-gather.3.cloned.1.call-done = bf16[1,65536,128]{2,1,0:T(8,128)(2,1)} async-done(((bf16[1,256,128]{2,1,0:T(8,128)(2,1)}), bf16[1,65536,128]{2,1,0:T(8,128)(2,1)}) %all-gather.3.cloned.1.call-update) | async-done | bytes 16777232 | tf_op jit(solution)/shard_map/all_gather | solution.py:33
  145.6 11.0 %constant_dynamic-update-slice_fusion.7 = (bf16[8,64,128]{2,1,0:T(8,128)(2,1)S(1)}, bf16[64,128]{1,0:T(8,128)(2,1)S(1)}) fusion(bf16[128,512,128]{2,1,0:T(8,128)(2,1)} %bitcast.56, s32[]{:T(128)S(6)} %select_n.115, bf16[128,64,128]{2,1,0:T(8,128)(2,1)S(1)} %all_to_all.5), kind=kOutput, calls=%fused_computation.49 | convolution fusion | flops 1082179584 | bytes 19038212 | tf_op jit(solution)/shard_map/dot_general | solution.py:72
  157.1 1.9 collective-permute-start.2
  159.0 1.9 collective-permute-start.3
  160.8 2.7 %collective-permute-start.4 = (bf16[64,128]{1,0:T(8,128)(2,1)S(1)}, bf16[64,128]{1,0:T(8,128)(2,1)S(1)}, u32[]{:S(2)}, u32[]{:S(2)}) collective-permute-start(bf16[64,128]{1,0:T(8,128)(2,1)S(1)} %get-tuple-element.16), channel_id=1, source_target_pairs={{0,32},{2,34},{4,36},{6,38},{8,40},{10,42},{12,44},{14,46},{16,48}... | collective-permute-start | bytes 49160 | tf_op jit(solution)/shard_map/ppermute | solution.py:16
  163.5 2.3 %collective-permute-start.5 = (bf16[64,128]{1,0:T(8,128)(2,1)S(1)}, bf16[64,128]{1,0:T(8,128)(2,1)S(1)}, u32[]{:S(2)}, u32[]{:S(2)}) collective-permute-start(bf16[64,128]{1,0:T(8,128)(2,1)S(1)} %get-tuple-element.16), channel_id=1, source_target_pairs={{0,40},{2,42},{4,44},{6,46},{8,48},{10,50},{12,52},{14,54},{16,56}... | collective-permute-start | bytes 49160 | tf_op jit(solution)/shard_map/ppermute | solution.py:16
  165.8 2.1 collective-permute-start.6
  168.0 0.8 collective-permute-start.7
  168.8 0.8 collective-permute-done.6
  169.6 1.0 collective-permute-done.7
  170.8 2.2 collective-permute-start.9
  173.0 1.2 collective-permute-start.10
  174.2 2.8 %collective-permute-done.8 = bf16[8,64,128]{2,1,0:T(8,128)(2,1)S(1)} collective-permute-done((bf16[8,64,128]{2,1,0:T(8,128)(2,1)S(1)}, bf16[8,64,128]{2,1,0:T(8,128)(2,1)S(1)}, u32[]{:S(2)}, u32[]{:S(2)}) %collective-permute-start.8) | collective-permute-done | bytes 131104 | tf_op jit(solution)/shard_map/ppermute | solution.py:16
  177.7 1.3 collective-permute-start.11
  179.0 1.7 collective-permute-start.12
  180.7 1.1 collective-permute-start.13
  181.8 5.0 %collective-permute-done.11 = bf16[4,8,64,128]{3,2,1,0:T(8,128)(2,1)S(1)} collective-permute-done((bf16[4,8,64,128]{3,2,1,0:T(8,128)(2,1)S(1)}, bf16[4,8,64,128]{3,2,1,0:T(8,128)(2,1)S(1)}, u32[]{:S(2)}, u32[]{:S(2)}) %collective-permute-start.11) | collective-permute-done | bytes 524320 | tf_op jit(solution)/shard_map/ppermute | solution.py:16
  186.8 3.0 %collective-permute-done.12 = bf16[4,8,64,128]{3,2,1,0:T(8,128)(2,1)S(1)} collective-permute-done((bf16[4,8,64,128]{3,2,1,0:T(8,128)(2,1)S(1)}, bf16[4,8,64,128]{3,2,1,0:T(8,128)(2,1)S(1)}, u32[]{:S(2)}, u32[]{:S(2)}) %collective-permute-start.12) | collective-permute-done | bytes 524320 | tf_op jit(solution)/shard_map/ppermute | solution.py:16
  189.8 15.8 %collective-permute-done.13 = bf16[4,8,64,128]{3,2,1,0:T(8,128)(2,1)S(1)} collective-permute-done((bf16[4,8,64,128]{3,2,1,0:T(8,128)(2,1)S(1)}, bf16[4,8,64,128]{3,2,1,0:T(8,128)(2,1)S(1)}, u32[]{:S(2)}, u32[]{:S(2)}) %collective-permute-start.13) | collective-permute-done | bytes 524320 | tf_op jit(solution)/shard_map/ppermute | solution.py:16
  205.9 1.7 fusion.25
  207.8 1.3 copy-done.2
  209.1 8.6 %subtract_convert_fusion = bf16[128,64,128]{2,1,0:T(8,128)(2,1)} fusion(f32[128,64,128]{2,1,0:T(8,128)} %get-tuple-element.8, f32[128,64,128]{2,1,0:T(8,128)S(1)} %copy-done.2, bf16[128,128,128]{2,0,1:T(8,128)(2,1)S(1)} %copy-done.1, bf16[128,64,128]{2,0,1:T(8,128)(2,1)S(1)} %fusion.25), kind=kOutput, calls=%fused_computation.9 | convolution fusion | flops 271581184 | bytes 16777216 | tf_op jit(solution)/shard_map/pca,pba->pcb/dot_general | solution.py:90
  (39 shorter events, 4.6 us)
Async XLA Ops:
  6.5 6.7 %copy-start = (bf16[8,128,128]{2,1,0:T(8,128)(2,1)S(1)}, bf16[8,128,128]{2,1,0:T(8,128)(2,1)}, u32[]{:S(2)}) copy-start(bf16[8,128,128]{2,1,0:T(8,128)(2,1)} %param.10) | copy-start | bytes 786436
  6.5 10.7 %copy-start.5 = (f32[128,128]{1,0:T(8,128)S(1)}, f32[128,128]{1,0:T(8,128)}, u32[]{:S(2)}) copy-start(f32[128,128]{1,0:T(8,128)} %param.13) | copy-start | bytes 196612
  6.5 10.7 %copy-start.3 = (bf16[128,64,128]{2,1,0:T(8,128)(2,1)S(1)}, bf16[128,64,128]{2,1,0:T(8,128)(2,1)}, u32[]{:S(2)}) copy-start(bf16[128,64,128]{2,1,0:T(8,128)(2,1)} %param.9) | copy-start | bytes 6291460
  6.5 139.0 %all-gather.3.cloned.1.call-start = ((), (), s32[]{:S(2)}) async-start(), calls=%async_computation.1 | async-start | bytes 16842752 | tf_op jit(solution)/shard_map/all_gather | solution.py:33
  7.3 14.7 %collective-permute-start = (bf16[128,64,128]{2,1,0:T(8,128)(2,1)}, bf16[128,64,128]{2,1,0:T(8,128)(2,1)}, u32[]{:S(2)}, u32[]{:S(2)}) collective-permute-start(bf16[128,64,128]{2,1,0:T(8,128)(2,1)} %param.8), channel_id=1, source_target_pairs={{0,1},{1,0},{2,3},{3,2},{4,5},{5,4},{6,7},{7,6},{8,9},{9,8},{10,11... | collective-permute-start | bytes 6291464 | tf_op jit(solution)/shard_map/ppermute | solution.py:36
  11.5 5.7 %copy-start.4 = (bf16[128,64,128]{2,1,0:T(8,128)(2,1)S(1)}, bf16[128,64,128]{2,1,0:T(8,128)(2,1)}, u32[]{:S(2)}) copy-start(bf16[128,64,128]{2,1,0:T(8,128)(2,1)} %param.8) | copy-start | bytes 6291460
  36.9 1.8 copy-start.6
  156.6 9.2 %collective-permute-start.1 = (bf16[64,128]{1,0:T(8,128)(2,1)S(1)}, bf16[64,128]{1,0:T(8,128)(2,1)S(1)}, u32[]{:S(2)}, u32[]{:S(2)}) collective-permute-start(bf16[64,128]{1,0:T(8,128)(2,1)S(1)} %get-tuple-element.16), channel_id=1, source_target_pairs={{0,8},{2,10},{4,12},{6,14},{8,16},{10,18},{12,20},{14,22},{16,24},... | collective-permute-start | bytes 49160 | tf_op jit(solution)/shard_map/ppermute | solution.py:16
  157.1 10.9 %collective-permute-start.2 = (bf16[64,128]{1,0:T(8,128)(2,1)S(1)}, bf16[64,128]{1,0:T(8,128)(2,1)S(1)}, u32[]{:S(2)}, u32[]{:S(2)}) collective-permute-start(bf16[64,128]{1,0:T(8,128)(2,1)S(1)} %get-tuple-element.16), channel_id=1, source_target_pairs={{0,16},{2,18},{4,20},{6,22},{8,24},{10,26},{12,28},{14,30},{16,32}... | collective-permute-start | bytes 49160 | tf_op jit(solution)/shard_map/ppermute | solution.py:16
  159.0 9.8 %collective-permute-start.3 = (bf16[64,128]{1,0:T(8,128)(2,1)S(1)}, bf16[64,128]{1,0:T(8,128)(2,1)S(1)}, u32[]{:S(2)}, u32[]{:S(2)}) collective-permute-start(bf16[64,128]{1,0:T(8,128)(2,1)S(1)} %get-tuple-element.16), channel_id=1, source_target_pairs={{0,24},{2,26},{4,28},{6,30},{8,32},{10,34},{12,36},{14,38},{16,40}... | collective-permute-start | bytes 49160 | tf_op jit(solution)/shard_map/ppermute | solution.py:16
  160.8 8.0 %collective-permute-start.4 = (bf16[64,128]{1,0:T(8,128)(2,1)S(1)}, bf16[64,128]{1,0:T(8,128)(2,1)S(1)}, u32[]{:S(2)}, u32[]{:S(2)}) collective-permute-start(bf16[64,128]{1,0:T(8,128)(2,1)S(1)} %get-tuple-element.16), channel_id=1, source_target_pairs={{0,32},{2,34},{4,36},{6,38},{8,40},{10,42},{12,44},{14,46},{16,48}... | collective-permute-start | bytes 49160 | tf_op jit(solution)/shard_map/ppermute | solution.py:16
  163.5 5.3 %collective-permute-start.5 = (bf16[64,128]{1,0:T(8,128)(2,1)S(1)}, bf16[64,128]{1,0:T(8,128)(2,1)S(1)}, u32[]{:S(2)}, u32[]{:S(2)}) collective-permute-start(bf16[64,128]{1,0:T(8,128)(2,1)S(1)} %get-tuple-element.16), channel_id=1, source_target_pairs={{0,40},{2,42},{4,44},{6,46},{8,48},{10,50},{12,52},{14,54},{16,56}... | collective-permute-start | bytes 49160 | tf_op jit(solution)/shard_map/ppermute | solution.py:16
  165.8 3.8 %collective-permute-start.6 = (bf16[64,128]{1,0:T(8,128)(2,1)S(1)}, bf16[64,128]{1,0:T(8,128)(2,1)S(1)}, u32[]{:S(2)}, u32[]{:S(2)}) collective-permute-start(bf16[64,128]{1,0:T(8,128)(2,1)S(1)} %get-tuple-element.16), channel_id=1, source_target_pairs={{0,48},{2,50},{4,52},{6,54},{8,56},{10,58},{12,60},{14,62},{16,0},... | collective-permute-start | bytes 49160 | tf_op jit(solution)/shard_map/ppermute | solution.py:16
  168.0 2.7 %collective-permute-start.7 = (bf16[64,128]{1,0:T(8,128)(2,1)S(1)}, bf16[64,128]{1,0:T(8,128)(2,1)S(1)}, u32[]{:S(2)}, u32[]{:S(2)}) collective-permute-start(bf16[64,128]{1,0:T(8,128)(2,1)S(1)} %get-tuple-element.16), channel_id=1, source_target_pairs={{0,56},{2,58},{4,60},{6,62},{8,0},{10,2},{12,4},{14,6},{16,8},{18,... | collective-permute-start | bytes 49160 | tf_op jit(solution)/shard_map/ppermute | solution.py:16
  170.6 6.4 %collective-permute-start.8 = (bf16[8,64,128]{2,1,0:T(8,128)(2,1)S(1)}, bf16[8,64,128]{2,1,0:T(8,128)(2,1)S(1)}, u32[]{:S(2)}, u32[]{:S(2)}) collective-permute-start(bf16[8,64,128]{2,1,0:T(8,128)(2,1)S(1)} %constant_dynamic-update-slice_fusion), channel_id=1, source_target_pairs={{0,2},{2,4},{4,6},{6,0},{8,10},{10,12},{12,14},{14,8},{16,18},{18,... | collective-permute-start | bytes 393224 | tf_op jit(solution)/shard_map/ppermute | solution.py:16
  170.8 6.3 %collective-permute-start.9 = (bf16[8,64,128]{2,1,0:T(8,128)(2,1)S(1)}, bf16[8,64,128]{2,1,0:T(8,128)(2,1)S(1)}, u32[]{:S(2)}, u32[]{:S(2)}) collective-permute-start(bf16[8,64,128]{2,1,0:T(8,128)(2,1)S(1)} %constant_dynamic-update-slice_fusion), channel_id=1, source_target_pairs={{0,4},{2,6},{4,0},{6,2},{8,12},{10,14},{12,8},{14,10},{16,20},{18,... | collective-permute-start | bytes 393224 | tf_op jit(solution)/shard_map/ppermute | solution.py:16
  173.0 4.6 %collective-permute-start.10 = (bf16[8,64,128]{2,1,0:T(8,128)(2,1)S(1)}, bf16[8,64,128]{2,1,0:T(8,128)(2,1)S(1)}, u32[]{:S(2)}, u32[]{:S(2)}) collective-permute-start(bf16[8,64,128]{2,1,0:T(8,128)(2,1)S(1)} %constant_dynamic-update-slice_fusion), channel_id=1, source_target_pairs={{0,6},{2,0},{4,2},{6,4},{8,14},{10,8},{12,10},{14,12},{16,22},{18,... | collective-permute-start | bytes 393224 | tf_op jit(solution)/shard_map/ppermute | solution.py:16
  177.7 9.1 %collective-permute-start.11 = (bf16[4,8,64,128]{3,2,1,0:T(8,128)(2,1)S(1)}, bf16[4,8,64,128]{3,2,1,0:T(8,128)(2,1)S(1)}, u32[]{:S(2)}, u32[]{:S(2)}) collective-permute-start(bf16[4,8,64,128]{3,2,1,0:T(8,128)(2,1)S(1)} %get-tuple-element.12), channel_id=1, source_target_pairs={{0,64},{2,66},{4,68},{6,70},{8,72},{10,74},{12,76},{14,78},{16,80}... | collective-permute-start | bytes 1572872 | tf_op jit(solution)/shard_map/ppermute | solution.py:16
  179.0 10.8 %collective-permute-start.12 = (bf16[4,8,64,128]{3,2,1,0:T(8,128)(2,1)S(1)}, bf16[4,8,64,128]{3,2,1,0:T(8,128)(2,1)S(1)}, u32[]{:S(2)}, u32[]{:S(2)}) collective-permute-start(bf16[4,8,64,128]{3,2,1,0:T(8,128)(2,1)S(1)} %get-tuple-element.12), channel_id=1, source_target_pairs={{0,128},{2,130},{4,132},{6,134},{8,136},{10,138},{12,140},{14,142}... | collective-permute-start | bytes 1572872 | tf_op jit(solution)/shard_map/ppermute | solution.py:16
  180.7 24.9 %collective-permute-start.13 = (bf16[4,8,64,128]{3,2,1,0:T(8,128)(2,1)S(1)}, bf16[4,8,64,128]{3,2,1,0:T(8,128)(2,1)S(1)}, u32[]{:S(2)}, u32[]{:S(2)}) collective-permute-start(bf16[4,8,64,128]{3,2,1,0:T(8,128)(2,1)S(1)} %get-tuple-element.12), channel_id=1, source_target_pairs={{0,192},{2,194},{4,196},{6,198},{8,200},{10,202},{12,204},{14,206}... | collective-permute-start | bytes 1572872 | tf_op jit(solution)/shard_map/ppermute | solution.py:16
  205.6 2.2 copy-start.1
  205.6 3.5 %copy-start.2 = (f32[128,64,128]{2,1,0:T(8,128)S(1)}, f32[128,64,128]{2,1,0:T(8,128)}, u32[]{:S(2)}) copy-start(f32[128,64,128]{2,1,0:T(8,128)} %get-tuple-element.10) | copy-start | bytes 12582916
Sparse Core Ops, SparseCore 0:
  11.0 134.4 all-gather.2
where the time goes:
time: 225 us
  blocking collectives  70.9 us (32%)
  waiting for transfers between devices  62.6 us (28%)
  matrix products  42 us (19%)
  starting transfers between devices  20.6 us (9%)
  between operations  13.5 us (6%)
  local copies, waits for them, and re-layouts  8.56 us (4%)
  other arithmetic  6.47 us (3%)
    all_to_all x1, blocking collectives, local(): incoming = lax.all_to_all(outgoing, 'pair', 0, 0, tiled=True)  70.9 us
    all_gather x1, waiting for transfers between devices, local(): lax.all_gather(factors[0], ('pair', 'aux'), axis=0, tiled=True)  32.9 us
    ppermute x13, waiting for transfers between devices, ring_gather(): pieces.append(lax.ppermute(block, 'pair', perm))  29 us
    ppermute x13, starting transfers between devices, ring_gather(): pieces.append(lax.ppermute(block, 'pair', perm))  19.8 us
    dot_general x1, matrix products, local(): jnp.einsum('pac,pab->pcb', margin, halfway, preferred_element_type=jnp.fl...  14.9 us
    dot_general x1, matrix products, local(): jnp.dot(dressed, own_factors, preferred_element_type=jnp.float32)  11 us
    dot_general x1, matrix products, local(): jnp.einsum('pca,pba->pcb', own_cycle, margin, preferred_element_type=jnp....  8.63 us
    div x1, other arithmetic, local(): inverse = 1.0 / denominator  4.77 us
  transfers between devices with their start and end apart: 15, of which 8 were waited for; matrix products, arithmetic and copies ran while one was open for 15% of the time, Pallas kernels for 0%

commit v1 on v0

--- a/solution.py
+++ b/solution.py
@@ -30,7 +30,12 @@
     aux_rows = factors.shape[1]
     ovl_count = margin_table.shape[0]
     cycle_scale = float(vir_width * aux_rows * aux_count * pair_count) ** (-0.5)
-    every_factor = lax.all_gather(factors[0], ("pair", "aux"), axis=0, tiled=True)
+    every_factor = jnp.concatenate(
+        lax.all_to_all(
+            jnp.stack([factors[0]] * lax.axis_size(("pair", "aux"))), ("pair", "aux"), 0, 0
+        ),
+        axis=0,
+    )
     every_factor = every_factor.reshape(axis_pairs, aux_count * aux_rows, vir_width)
     own_factors = lax.dynamic_index_in_dim(every_factor, own_index, 0, keepdims=False)
     other_amp = lax.ppermute(amplitudes, "aux", perm=[(0, 1), (1, 0)])

time: 225 us -> 555 us (2.47)
  blocking collectives: 70.9 us -> 440 us
  waiting for transfers between devices: 62.6 us -> 34.1 us
  between operations: 13.5 us -> 0.15 us
    all_to_all x0 -> x1, blocking collectives: none -> 376 us  [local(): lax.all_to_all(jnp.stack([factors[0]] * lax.axis_size(('pair', 'aux'))),...]
    all_gather x1 -> x0, waiting for transfers between devices: 32.9 us -> none  [local(): lax.all_gather(factors[0], ('pair', 'aux'), axis=0, tiled=True)]
    all_to_all x1, blocking collectives: 70.9 us -> 64.2 us  [local(): incoming = lax.all_to_all(outgoing, 'pair', 0, 0, tiled=True)]
  transfers between devices with their start and end apart: 15 -> 14, of which waited for: 8 -> 8; matrix products, arithmetic and copies ran while one was open for 15% -> 3% of each run, Pallas kernels for 0% -> 0%
where the time goes in v1:
time: 555 us; the launch traced here: 553 us
  blocking collectives  440 us (79%)
  matrix products  42.1 us (8%)
  waiting for transfers between devices  34.1 us (6%)
  starting transfers between devices  17.1 us (3%)
  local copies, waits for them, and re-layouts  12.8 us (2%)
  other arithmetic  6.48 us (1%)
    all_to_all x1, blocking collectives, local(): lax.all_to_all(jnp.stack([factors[0]] * lax.axis_size(('pair', 'aux'))),...  376 us
    all_to_all x1, blocking collectives, local(): incoming = lax.all_to_all(outgoing, 'pair', 0, 0, tiled=True)  64.2 us
    ppermute x13, waiting for transfers between devices, ring_gather(): pieces.append(lax.ppermute(block, 'pair', perm))  34.1 us
    ppermute x13, starting transfers between devices, ring_gather(): pieces.append(lax.ppermute(block, 'pair', perm))  16.3 us
    dot_general x1, matrix products, local(): jnp.einsum('pac,pab->pcb', margin, halfway, preferred_element_type=jnp.fl...  14.9 us
  transfers between devices with their start and end apart: 14, of which 8 were waited for; matrix products, arithmetic and copies ran while one was open for 3% of the time, Pallas kernels for 0%

profile of v1, /device:TPU:3, one launch (start us, length us, event | category | flops | bytes accessed | tf_op | source)
XLA Modules:
  0.0 552.6 jit_solution(10277231326709480183)
XLA Ops:
  0.0 0.8 collective-permute-start
  0.8 1.2 dynamic_slice.15
  2.7 1.6 gather_fusion
  4.3 1.1 constant_dynamic-slice_fusion
  6.0 3.9 convolution_convert_fusion
  10.0 4.8 subtract_divide_fusion
  14.7 14.9 %fusion.6 = bf16[128,128,128]{2,1,0:T(8,128)(2,1)} fusion(bf16[128,128,128]{2,0,1:T(8,128)(2,1)} %convolution_convert_fusion, bf16[128,64,128]{2,1,0:T(8,128)(2,1)} %collective-permute-done, bf16[128,64,128]{2,1,0:T(8,128)(2,1)} %param.8, pred[]{:T(512)S(6)} %eq.62), kind=kOutput, calls=%fused_computation.12 | convolution fusion | flops 1094713344 | bytes 12582913 | tf_op jit(solution)/shard_map/pac,pab->pcb/dot_general | solution.py:56
  29.7 1.8 dynamic-slice_convert_fusion
  31.5 1.8 fusion.22
  33.3 1.4 copy.17
  34.6 64.2 %all_to_all.10 = bf16[128,64,128]{2,1,0:T(8,128)(2,1)S(1)} all-to-all(bf16[128,64,128]{2,1,0:T(8,128)(2,1)S(1)} %copy.17), channel_id=1, replica_groups=mesh['pair'=128,'aux'=2] {'pair'}, dimensions={0} | all-to-all | bytes 4194304 | tf_op jit(solution)/shard_map/all_to_all | solution.py:73
  98.8 4.3 stack.60
  103.1 375.7 %all_to_all.11 = bf16[256,256,128]{2,1,0:T(8,128)(2,1)} all-to-all(bf16[256,256,128]{2,1,0:T(8,128)(2,1)S(1)} %stack.60), channel_id=1, replica_groups=mesh['pair'=128,'aux'=2] {'pair','aux'}, dimensions={0} | all-to-all | bytes 33554432 | tf_op jit(solution)/shard_map/all_to_all | solution.py:34
  478.7 11.0 %constant_dynamic-update-slice_fusion.7 = (bf16[8,64,128]{2,1,0:T(8,128)(2,1)S(1)}, bf16[64,128]{1,0:T(8,128)(2,1)S(1)}) fusion(bf16[128,512,128]{2,1,0:T(8,128)(2,1)} %bitcast.57, s32[]{:T(128)S(6)} %select_n.115, bf16[128,64,128]{2,1,0:T(8,128)(2,1)S(1)} %all_to_all.10), kind=kOutput, calls=%fused_computation.49 | convolution fusion | flops 1082179584 | bytes 19038212 | tf_op jit(solution)/shard_map/dot_general | solution.py:77
  490.3 4.1 collective-permute-start.5
  494.4 3.5 collective-permute-start.4
  498.2 1.0 collective-permute-start.2
  499.1 3.8 collective-permute-done.2
  503.0 2.0 collective-permute-start.7
  505.0 1.6 collective-permute-done.7
  506.6 1.6 collective-permute-start.10
  509.0 2.6 collective-permute-done.10
  511.6 2.1 collective-permute-done.9
  513.7 1.3 collective-permute-done.8
  515.1 1.1 collective-permute-start.12
  516.2 1.6 collective-permute-start.11
  517.8 7.2 %collective-permute-done.12 = bf16[4,8,64,128]{3,2,1,0:T(8,128)(2,1)S(1)} collective-permute-done((bf16[4,8,64,128]{3,2,1,0:T(8,128)(2,1)S(1)}, bf16[4,8,64,128]{3,2,1,0:T(8,128)(2,1)S(1)}, u32[]{:S(2)}, u32[]{:S(2)}) %collective-permute-start.12) | collective-permute-done | bytes 524320 | tf_op jit(solution)/shard_map/ppermute | solution.py:16
  525.0 13.4 %collective-permute-done.11 = bf16[4,8,64,128]{3,2,1,0:T(8,128)(2,1)S(1)} collective-permute-done((bf16[4,8,64,128]{3,2,1,0:T(8,128)(2,1)S(1)}, bf16[4,8,64,128]{3,2,1,0:T(8,128)(2,1)S(1)}, u32[]{:S(2)}, u32[]{:S(2)}) %collective-permute-start.11) | collective-permute-done | bytes 524320 | tf_op jit(solution)/shard_map/ppermute | solution.py:16
  538.4 2.0 collective-permute-done.13
  540.7 1.7 fusion.25
  542.6 1.3 copy-done.3
  543.9 8.7 %subtract_convert_fusion = bf16[128,64,128]{2,1,0:T(8,128)(2,1)} fusion(f32[128,64,128]{2,1,0:T(8,128)} %get-tuple-element.8, f32[128,64,128]{2,1,0:T(8,128)S(1)} %copy-done.3, bf16[128,128,128]{2,0,1:T(8,128)(2,1)S(1)} %copy-done.2, bf16[128,64,128]{2,0,1:T(8,128)(2,1)S(1)} %fusion.25), kind=kOutput, calls=%fused_computation.9 | convolution fusion | flops 271581184 | bytes 16777216 | tf_op jit(solution)/shard_map/pca,pba->pcb/dot_general | solution.py:95
  (42 shorter events, 3.4 us)
Async XLA Ops:
  0.0 6.0 %copy-start = (bf16[8,128,128]{2,1,0:T(8,128)(2,1)S(1)}, bf16[8,128,128]{2,1,0:T(8,128)(2,1)}, u32[]{:S(2)}) copy-start(bf16[8,128,128]{2,1,0:T(8,128)(2,1)} %param.10) | copy-start | bytes 786436
  0.0 10.0 %copy-start.6 = (f32[128,128]{1,0:T(8,128)S(1)}, f32[128,128]{1,0:T(8,128)}, u32[]{:S(2)}) copy-start(f32[128,128]{1,0:T(8,128)} %param.13) | copy-start | bytes 196612
  0.0 10.0 %copy-start.4 = (bf16[128,64,128]{2,1,0:T(8,128)(2,1)S(1)}, bf16[128,64,128]{2,1,0:T(8,128)(2,1)}, u32[]{:S(2)}) copy-start(bf16[128,64,128]{2,1,0:T(8,128)(2,1)} %param.9) | copy-start | bytes 6291460
  0.0 14.7 %collective-permute-start = (bf16[128,64,128]{2,1,0:T(8,128)(2,1)}, bf16[128,64,128]{2,1,0:T(8,128)(2,1)}, u32[]{:S(2)}, u32[]{:S(2)}) collective-permute-start(bf16[128,64,128]{2,1,0:T(8,128)(2,1)} %param.8), channel_id=1, source_target_pairs={{0,1},{1,0},{2,3},{3,2},{4,5},{5,4},{6,7},{7,6},{8,9},{9,8},{10,11... | collective-permute-start | bytes 6291464 | tf_op jit(solution)/shard_map/ppermute | solution.py:41
  4.3 5.7 %copy-start.5 = (bf16[128,64,128]{2,1,0:T(8,128)(2,1)S(1)}, bf16[128,64,128]{2,1,0:T(8,128)(2,1)}, u32[]{:S(2)}) copy-start(bf16[128,64,128]{2,1,0:T(8,128)(2,1)} %param.8) | copy-start | bytes 6291460
  29.7 1.8 copy-start.8
  33.2 65.6 %copy-start.7 = (bf16[1,256,128]{2,1,0:T(8,128)(2,1)S(1)}, bf16[1,256,128]{2,1,0:T(8,128)(2,1)}, u32[]{:S(2)}) copy-start(bf16[1,256,128]{2,1,0:T(8,128)(2,1)} %param.12) | copy-start | bytes 196612
  489.8 8.4 %collective-permute-start.1 = (bf16[64,128]{1,0:T(8,128)(2,1)S(1)}, bf16[64,128]{1,0:T(8,128)(2,1)S(1)}, u32[]{:S(2)}, u32[]{:S(2)}) collective-permute-start(bf16[64,128]{1,0:T(8,128)(2,1)S(1)} %get-tuple-element.16), channel_id=1, source_target_pairs={{0,8},{2,10},{4,12},{6,14},{8,16},{10,18},{12,20},{14,22},{16,24},... | collective-permute-start | bytes 49160 | tf_op jit(solution)/shard_map/ppermute | solution.py:16
  489.9 15.1 %collective-permute-start.6 = (bf16[64,128]{1,0:T(8,128)(2,1)S(1)}, bf16[64,128]{1,0:T(8,128)(2,1)S(1)}, u32[]{:S(2)}, u32[]{:S(2)}) collective-permute-start(bf16[64,128]{1,0:T(8,128)(2,1)S(1)} %get-tuple-element.16), channel_id=1, source_target_pairs={{0,48},{2,50},{4,52},{6,54},{8,56},{10,58},{12,60},{14,62},{16,0},... | collective-permute-start | bytes 49160 | tf_op jit(solution)/shard_map/ppermute | solution.py:16
  490.3 14.7 %collective-permute-start.5 = (bf16[64,128]{1,0:T(8,128)(2,1)S(1)}, bf16[64,128]{1,0:T(8,128)(2,1)S(1)}, u32[]{:S(2)}, u32[]{:S(2)}) collective-permute-start(bf16[64,128]{1,0:T(8,128)(2,1)S(1)} %get-tuple-element.16), channel_id=1, source_target_pairs={{0,40},{2,42},{4,44},{6,46},{8,48},{10,50},{12,52},{14,54},{16,56}... | collective-permute-start | bytes 49160 | tf_op jit(solution)/shard_map/ppermute | solution.py:16
  494.4 10.5 %collective-permute-start.4 = (bf16[64,128]{1,0:T(8,128)(2,1)S(1)}, bf16[64,128]{1,0:T(8,128)(2,1)S(1)}, u32[]{:S(2)}, u32[]{:S(2)}) collective-permute-start(bf16[64,128]{1,0:T(8,128)(2,1)S(1)} %get-tuple-element.16), channel_id=1, source_target_pairs={{0,32},{2,34},{4,36},{6,38},{8,40},{10,42},{12,44},{14,46},{16,48}... | collective-permute-start | bytes 49160 | tf_op jit(solution)/shard_map/ppermute | solution.py:16
  497.9 7.0 %collective-permute-start.3 = (bf16[64,128]{1,0:T(8,128)(2,1)S(1)}, bf16[64,128]{1,0:T(8,128)(2,1)S(1)}, u32[]{:S(2)}, u32[]{:S(2)}) collective-permute-start(bf16[64,128]{1,0:T(8,128)(2,1)S(1)} %get-tuple-element.16), channel_id=1, source_target_pairs={{0,24},{2,26},{4,28},{6,30},{8,32},{10,34},{12,36},{14,38},{16,40}... | collective-permute-start | bytes 49160 | tf_op jit(solution)/shard_map/ppermute | solution.py:16
  498.2 4.8 collective-permute-start.2
  503.0 3.7 collective-permute-start.7
  506.6 4.9 collective-permute-start.10
  508.2 5.4 collective-permute-start.9
  509.0 6.0 %collective-permute-start.8 = (bf16[8,64,128]{2,1,0:T(8,128)(2,1)S(1)}, bf16[8,64,128]{2,1,0:T(8,128)(2,1)S(1)}, u32[]{:S(2)}, u32[]{:S(2)}) collective-permute-start(bf16[8,64,128]{2,1,0:T(8,128)(2,1)S(1)} %constant_dynamic-update-slice_fusion), channel_id=1, source_target_pairs={{0,2},{2,4},{4,6},{6,0},{8,10},{10,12},{12,14},{14,8},{16,18},{18,... | collective-permute-start | bytes 393224 | tf_op jit(solution)/shard_map/ppermute | solution.py:16
  515.1 9.9 %collective-permute-start.12 = (bf16[4,8,64,128]{3,2,1,0:T(8,128)(2,1)S(1)}, bf16[4,8,64,128]{3,2,1,0:T(8,128)(2,1)S(1)}, u32[]{:S(2)}, u32[]{:S(2)}) collective-permute-start(bf16[4,8,64,128]{3,2,1,0:T(8,128)(2,1)S(1)} %get-tuple-element.12), channel_id=1, source_target_pairs={{0,128},{2,130},{4,132},{6,134},{8,136},{10,138},{12,140},{14,142}... | collective-permute-start | bytes 1572872 | tf_op jit(solution)/shard_map/ppermute | solution.py:16
  516.2 22.3 %collective-permute-start.11 = (bf16[4,8,64,128]{3,2,1,0:T(8,128)(2,1)S(1)}, bf16[4,8,64,128]{3,2,1,0:T(8,128)(2,1)S(1)}, u32[]{:S(2)}, u32[]{:S(2)}) collective-permute-start(bf16[4,8,64,128]{3,2,1,0:T(8,128)(2,1)S(1)} %get-tuple-element.12), channel_id=1, source_target_pairs={{0,64},{2,66},{4,68},{6,70},{8,72},{10,74},{12,76},{14,78},{16,80}... | collective-permute-start | bytes 1572872 | tf_op jit(solution)/shard_map/ppermute | solution.py:16
  517.7 22.7 %collective-permute-start.13 = (bf16[4,8,64,128]{3,2,1,0:T(8,128)(2,1)S(1)}, bf16[4,8,64,128]{3,2,1,0:T(8,128)(2,1)S(1)}, u32[]{:S(2)}, u32[]{:S(2)}) collective-permute-start(bf16[4,8,64,128]{3,2,1,0:T(8,128)(2,1)S(1)} %get-tuple-element.12), channel_id=1, source_target_pairs={{0,192},{2,194},{4,196},{6,198},{8,200},{10,202},{12,204},{14,206}... | collective-permute-start | bytes 1572872 | tf_op jit(solution)/shard_map/ppermute | solution.py:16
  540.4 2.2 copy-start.2
  540.4 3.5 copy-start.3
  543.9 8.7 %copy-start.1 = (bf16[8,128,128]{2,1,0:T(8,128)(2,1)S(1)}, bf16[8,128,128]{2,1,0:T(8,128)(2,1)}, u32[]{:S(2)}) copy-start(bf16[8,128,128]{2,1,0:T(8,128)(2,1)} %param.10) | copy-start | bytes 786436
